TPU v7x, 256 devices: a whole 4x4x8 slice. The times are simulated.
256 devices in a mesh: space: 16 (over x_hi, z), chan: 8 (over y, core), dp: 2 (over x_lo).
Axes of the slice: x: 4 (x_hi: 2, x_lo: 2; x = x_hi * 2 + x_lo), y: 4, z: 8, core: 2. Of those that a mesh axis runs over, the one named last changes fastest.
Arguments:
- inputs: bfloat16 [2, 32, 8, 128, 512], P('dp', 'space', None, 'chan'), may hold values from -6 to 6
- cotangent: bfloat16 [2, 32, 8, 128, 512], P('dp', 'space', None, 'chan'), may hold values from -6 to 6
- weight: bfloat16 [27, 128, 128], P(None, 'chan'), may hold values from -0.109375 to 0.109375
Outputs:
- input_grad: bfloat16 [2, 32, 8, 128, 512], P('dp', 'space', None, 'chan')
- weight_grad: float32 [27, 128, 128], P(None, 'chan')
All inputs are finite; a program needn't handle non-finite values.
Results may differ from a plain program's by a relative error of at most 0.001.
Values may be sent and summed in bfloat16 or wider, within the bound.
No kernel may reach another device: no remote copies, remote signals or barrier semaphores. Data moves between devices by JAX's collectives and lax.ppermute only.
A program may use at most 64 MiB of HBM per device.

v0:
```python
import math

import jax
import jax.numpy as jnp
from jax import lax
from jax.sharding import PartitionSpec as P


def from_behind(value, axis, steps):
    count = lax.axis_size(axis)
    initial, last = (max(0, -steps), min(count, count - steps))
    return lax.ppermute(value, axis, [(source, source + steps) for source in range(initial, last)])


def shift_cells(block, step_z, step_y):
    zero = jnp.zeros((), block.dtype)
    config = ((0, 0, 0), (0, 0, 0), (step_z, -step_z, 0), (0, 0, 0), (step_y, -step_y, 0))
    return lax.pad(block, zero, config)


def local(inputs, cotangent, weight):
    samples, planes, depth, channels, width = inputs.shape
    outputs = weight.shape[2]
    gathered = lax.all_gather(cotangent, "chan", axis=3, tiled=True)
    lower_plane = from_behind(gathered[:, -1:], "space", 1)
    upper_plane = from_behind(gathered[:, :1], "space", -1)
    stacked = jnp.concatenate(
        [shift_cells(inputs, -step_z, -step_y) for step_z in (-1, 0, 1) for step_y in (-1, 0, 1)],
        axis=3,
    )
    accum = jnp.zeros(inputs.shape, jnp.float32)
    groups = []
    for step_x in (-1, 0, 1):
        if step_x == 1:
            slab = jnp.concatenate([lower_plane, gathered[:, : planes - 1]], axis=1)
        elif step_x == -1:
            slab = jnp.concatenate([gathered[:, 1:], upper_plane], axis=1)
        else:
            slab = gathered
        first = 9 * (step_x + 1)
        groups.append(
            jnp.einsum("bxzky,bxzcy->kc", stacked, slab, preferred_element_type=jnp.float32)
        )
        for step_y in (-1, 0, 1):
            kernel = weight[first + step_y + 1 : first + 9 : 3].reshape(3 * channels, outputs)
            product = jnp.einsum(
                "bxzcy,kc->bxzky", slab, kernel, preferred_element_type=jnp.float32
            )
            for place, step_z in enumerate((-1, 0, 1)):
                part = product[:, :, :, place * channels : (place + 1) * channels]
                accum = accum + shift_cells(part, step_z, step_y)
    input_grad = accum.astype(jnp.bfloat16)
    local_grad = jnp.concatenate(groups, axis=0).reshape(27, channels, outputs)
    count = samples * lax.axis_size("dp") * planes * lax.axis_size("space") * depth * width
    scale = 1.0 / math.sqrt(count)
    weight_grad = lax.psum(local_grad, ("space", "dp")) * scale
    return (input_grad, weight_grad)


def solution(mesh):
    placed = (
        P("dp", "space", None, "chan", None),
        P("dp", "space", None, "chan", None),
        P(None, "chan", None),
    )
    return jax.shard_map(
        local,
        mesh=mesh,
        in_specs=placed,
        out_specs=(P("dp", "space", None, "chan", None), P(None, "chan", None)),
        check_vma=False,
    )
```

profile of v0, /device:TPU:4, one launch (start us, length us, event | category | flops | bytes accessed | tf_op | source)
XLA Modules:
  0.0 231.8 jit_solution(5952417123900889191)
XLA Ops:
  7.2 0.7 all-gather.2.cloned.1.call-update
  8.0 1.1 fusion.64
  9.0 1.0 fusion.60
  10.0 1.1 fusion.65
  11.1 1.1 fusion.62
  12.7 1.4 copy-done.5
  14.2 26.5 %all-gather.2.cloned.1.call-done = bf16[1,2,8,128,512]{4,3,2,1,0:T(8,128)(2,1)} async-done(((bf16[1,2,8,16,512]{4,3,2,1,0:T(8,128)(2,1)}), bf16[1,2,8,128,512]{4,3,2,1,0:T(8,128)(2,1)}) %all-gather.2.cloned.1.call-update) | async-done | bytes 2097168 | tf_op jit(solution)/shard_map/all_gather | solution.py:24
  40.7 1.9 fusion.68
  42.6 3.5 %collective-permute-start.1 = (bf16[1,1,8,128,512]{4,3,2,1,0:T(8,128)(2,1)S(1)}, bf16[1,1,8,128,512]{4,3,2,1,0:T(8,128)(2,1)S(1)}, u32[]{:S(2)}, u32[]{:S(2)}) collective-permute-start(bf16[1,1,8,128,512]{4,3,2,1,0:T(8,128)(2,1)S(1)} %get-tuple-element.2), channel_id=1, source_target_pairs={{0,16},{16,32},{32,48},{48,64},{64,80},{80,96},{96,112},{112,128},... | collective-permute-start | bytes 3145736 | tf_op jit(solution)/shard_map/ppermute | solution.py:12
  46.0 6.0 %collective-permute-start = (bf16[1,1,8,128,512]{4,3,2,1,0:T(8,128)(2,1)S(1)}, bf16[1,1,8,128,512]{4,3,2,1,0:T(8,128)(2,1)S(1)}, u32[]{:S(2)}, u32[]{:S(2)}) collective-permute-start(bf16[1,1,8,128,512]{4,3,2,1,0:T(8,128)(2,1)S(1)} %get-tuple-element.3), channel_id=1, source_target_pairs={{16,0},{32,16},{48,32},{64,48},{80,64},{96,80},{112,96},{128,112},... | collective-permute-start | bytes 3145736 | tf_op jit(solution)/shard_map/ppermute | solution.py:12
  52.0 0.4 fusion.16
  52.5 0.4 fusion.19
  52.9 0.4 fusion.13
  53.6 1.5 fusion.72
  55.2 1.2 fusion.74
  56.3 1.1 copy-done.6
  57.4 0.8 fusion.25
  58.2 16.4 %collective-permute-done = bf16[1,1,8,128,512]{4,3,2,1,0:T(8,128)(2,1)S(1)} collective-permute-done((bf16[1,1,8,128,512]{4,3,2,1,0:T(8,128)(2,1)S(1)}, bf16[1,1,8,128,512]{4,3,2,1,0:T(8,128)(2,1)S(1)}, u32[]{:S(2)}, u32[]{:S(2)}) %collective-permute-start) | collective-permute-done | bytes 1048608 | tf_op jit(solution)/shard_map/ppermute | solution.py:12
  74.5 0.4 convolution_bitcast_fusion.3
  75.0 1.2 fusion.71
  76.2 0.4 convolution_bitcast_fusion
  76.6 1.2 fusion.77
  77.8 0.8 fusion.30
  78.6 0.8 fusion.22
  79.4 0.7 pad_maximum_fusion
  80.1 1.7 convolution_bitcast_fusion.4
  81.8 0.4 convolution_bitcast_fusion.5
  82.6 0.4 convolution_bitcast_fusion.1
  83.1 0.4 convolution_bitcast_fusion.2
  86.3 4.3 %fusion.59 = bf16[1,2,8,16,512]{4,3,2,1,0:T(8,128)(2,1)} fusion(f32[1,2,8,16,512]{4,3,2,1,0:T(8,128)S(1)} %copy-done.19, f32[1,2,8,16,512]{4,3,2,1,0:T(8,128)S(1)} %copy-done.20, f32[1,2,8,16,512]{4,3,2,1,0:T(8,128)S(1)} %copy-done.18, f32[1,2,8,16,512]{4,3,2,1,0:T(8,128)S(1)} %get-tuple-element.41, f32[1,2,8,48,512]{4,3,2,1,0:T(8,128)S(1)} %convolution_bitcast_fusion.1, ...), kind=kLoop, calls=%fused_computation.77 | loop fusion | flops 3538944 | bytes 14417920 | tf_op jit(solution)/shard_map/convert_element_type | solution.py:52
  90.6 132.7 %all-reduce.34.cloned.1.call-done = f32[27,16,128]{2,1,0:T(8,128)} async-done(((f32[27,16,128]{2,1,0:T(8,128)}), f32[27,16,128]{2,1,0:T(8,128)}) %all-reduce.34.cloned.1.call-update) | async-done | bytes 221200 | tf_op jit(solution)/shard_map/psum | solution.py:56
  223.3 1.6 broadcast_multiply_fusion
  (54 shorter events, 3.9 us)
Async XLA Ops:
  7.2 5.1 %copy-start.1 = (bf16[1,2,8,16,512]{4,3,2,1,0:T(8,128)(2,1)S(1)}, bf16[1,2,8,16,512]{4,3,2,1,0:T(8,128)(2,1)}, u32[]{:S(2)}) copy-start(bf16[1,2,8,16,512]{4,3,2,1,0:T(8,128)(2,1)} %param.3) | copy-start | bytes 786436
  7.2 33.5 %all-gather.2.cloned.1.call-start = ((), (), s32[]{:S(2)}) async-start(), calls=%async_computation | async-start | bytes 2359296 | tf_op jit(solution)/shard_map/all_gather | solution.py:24
  7.9 215.4 %all-reduce.34.cloned.1.call-start = ((), (), s32[]{:S(2)}) async-start(), calls=%async_computation.1 | async-start | bytes 442368 | tf_op jit(solution)/shard_map/psum | solution.py:56
  9.0 5.1 %copy-start.21 = (bf16[27,16,128]{2,1,0:T(8,128)(2,1)S(1)}, bf16[27,16,128]{2,1,0:T(8,128)(2,1)}, u32[]{:S(2)}) copy-start(bf16[27,16,128]{2,1,0:T(8,128)(2,1)} %param.5) | copy-start | bytes 331780
  12.7 1.4 copy-start.5
  40.7 11.4 %copy-start = (bf16[1,2,8,128,512]{4,3,2,1,0:T(8,128)(2,1)S(1)}, bf16[1,2,8,128,512]{4,3,2,1,0:T(8,128)(2,1)}, u32[]{:S(2)}) copy-start(bf16[1,2,8,128,512]{4,3,2,1,0:T(8,128)(2,1)} %all-gather.2.cloned.1.call-done) | copy-start | bytes 6291460
  42.6 33.6 %collective-permute-start.1 = (bf16[1,1,8,128,512]{4,3,2,1,0:T(8,128)(2,1)S(1)}, bf16[1,1,8,128,512]{4,3,2,1,0:T(8,128)(2,1)S(1)}, u32[]{:S(2)}, u32[]{:S(2)}) collective-permute-start(bf16[1,1,8,128,512]{4,3,2,1,0:T(8,128)(2,1)S(1)} %get-tuple-element.2), channel_id=1, source_target_pairs={{0,16},{16,32},{32,48},{48,64},{64,80},{80,96},{96,112},{112,128},... | collective-permute-start | bytes 3145736 | tf_op jit(solution)/shard_map/ppermute | solution.py:12
  46.0 28.5 %collective-permute-start = (bf16[1,1,8,128,512]{4,3,2,1,0:T(8,128)(2,1)S(1)}, bf16[1,1,8,128,512]{4,3,2,1,0:T(8,128)(2,1)S(1)}, u32[]{:S(2)}, u32[]{:S(2)}) collective-permute-start(bf16[1,1,8,128,512]{4,3,2,1,0:T(8,128)(2,1)S(1)} %get-tuple-element.3), channel_id=1, source_target_pairs={{16,0},{32,16},{48,32},{64,48},{80,64},{96,80},{112,96},{128,112},... | collective-permute-start | bytes 3145736 | tf_op jit(solution)/shard_map/ppermute | solution.py:12
  52.5 1.2 copy-start.4
  55.2 2.2 copy-start.6
  74.5 4.0 %copy-start.2 = (bf16[1,1,8,128,512]{4,3,2,1,0:T(8,128)(2,1)}, bf16[1,1,8,128,512]{4,3,2,1,0:T(8,128)(2,1)S(1)}, u32[]{:S(2)}) copy-start(bf16[1,1,8,128,512]{4,3,2,1,0:T(8,128)(2,1)S(1)} %collective-permute-done) | copy-start | bytes 3145732
  80.1 1.8 copy-start.3
  83.1 1.0 copy-start.17
  83.1 1.2 copy-start.18
  83.1 1.3 copy-start.19
  83.1 1.5 copy-start.20
  83.5 1.3 copy-start.7
  83.5 1.5 copy-start.8
  83.5 1.6 copy-start.9
  83.5 1.8 copy-start.10
  83.6 1.9 copy-start.11
  83.6 2.1 copy-start.12
  83.6 2.2 copy-start.13
  83.6 2.4 %copy-start.14 = (f32[1,2,8,16,512]{4,3,2,1,0:T(8,128)S(1)}, f32[1,2,8,16,512]{4,3,2,1,0:T(8,128)}, u32[]{:S(2)}) copy-start(f32[1,2,8,16,512]{4,3,2,1,0:T(8,128)} %get-tuple-element.19) | copy-start | bytes 1572868
  83.6 2.5 %copy-start.15 = (f32[1,2,8,16,512]{4,3,2,1,0:T(8,128)S(1)}, f32[1,2,8,16,512]{4,3,2,1,0:T(8,128)}, u32[]{:S(2)}) copy-start(f32[1,2,8,16,512]{4,3,2,1,0:T(8,128)} %get-tuple-element.9) | copy-start | bytes 1572868
  83.6 2.7 %copy-start.16 = (f32[1,2,8,16,512]{4,3,2,1,0:T(8,128)S(1)}, f32[1,2,8,16,512]{4,3,2,1,0:T(8,128)}, u32[]{:S(2)}) copy-start(f32[1,2,8,16,512]{4,3,2,1,0:T(8,128)} %get-tuple-element.10) | copy-start | bytes 1572868
Sparse Core Ops, SparseCore 0:
  9.8 30.7 all-gather.1
  80.2 143.0 all-reduce.33
where the time goes:
time: 232 us
  waiting for transfers between devices  176 us (76%)
  local copies, waits for them, and re-layouts  17.5 us (8%)
  between operations  14.4 us (6%)
  starting transfers between devices  9.53 us (4%)
  matrix products  7.39 us (3%)
  other arithmetic  6.63 us (3%)
    psum x1, waiting for transfers between devices, local(): weight_grad = lax.psum(local_grad, ('space', 'dp')) * scale  133 us
    all_gather x1, waiting for transfers between devices, local(): gathered = lax.all_gather(cotangent, 'chan', axis=3, tiled=True)  26.5 us
    ppermute x2, waiting for transfers between devices, from_behind(): lax.ppermute(value, axis, [(source, source + steps) for source in range(i...  16.4 us
    unnamed x52, local copies, waits for them, and re-layouts  9.68 us
    ppermute x2, starting transfers between devices, from_behind(): lax.ppermute(value, axis, [(source, source + steps) for source in range(i...  9.46 us
    slice x6, local copies, waits for them, and re-layouts, local(): part = product[:, :, :, place * channels:(place + 1) * channels]  5.81 us
    dot_general x9, matrix products, local(): jnp.einsum('bxzcy,kc->bxzky', slab, kernel, preferred_element_type=jnp.fl...  5.09 us
  transfers between devices with their start and end apart: 4, of which 3 were waited for; matrix products, arithmetic and copies ran while one was open for 8% of the time, Pallas kernels for 0%

commit v1 on v0

--- a/solution.py
+++ b/solution.py
@@ -10,6 +10,18 @@
     count = lax.axis_size(axis)
     initial, last = (max(0, -steps), min(count, count - steps))
     return lax.ppermute(value, axis, [(source, source + steps) for source in range(initial, last)])
+
+
+def exchange_sum(value, axis, distance):
+    count = lax.axis_size(axis)
+    return value + lax.ppermute(value, axis, [(i, i ^ distance) for i in range(count)])
+
+
+def butterfly_sum(value):
+    value = exchange_sum(value, "dp", 1)
+    for distance in (1, 8, 2, 4):
+        value = exchange_sum(value, "space", distance)
+    return value
 
 
 def shift_cells(block, step_z, step_y):
@@ -53,7 +65,7 @@
     local_grad = jnp.concatenate(groups, axis=0).reshape(27, channels, outputs)
     count = samples * lax.axis_size("dp") * planes * lax.axis_size("space") * depth * width
     scale = 1.0 / math.sqrt(count)
-    weight_grad = lax.psum(local_grad, ("space", "dp")) * scale
+    weight_grad = butterfly_sum(local_grad) * scale
     return (input_grad, weight_grad)
 
 

time: 232 us -> 136 us (0.59)
  waiting for transfers between devices: 176 us -> 93.1 us
  local copies, waits for them, and re-layouts: 17.5 us -> 8.23 us
  other arithmetic: 6.63 us -> 4.23 us
    psum x1 -> x0, waiting for transfers between devices: 133 us -> none  [local(): weight_grad = lax.psum(local_grad, ('space', 'dp')) * scale]
    ppermute x0 -> x5, waiting for transfers between devices: none -> 39.2 us  [exchange_sum(): lax.ppermute(value, axis, [(i, i ^ distance) for i in range(count)])]
    ppermute x2, waiting for transfers between devices: 16.4 us -> 25.3 us  [from_behind(): lax.ppermute(value, axis, [(source, source + steps) for source in range(i...]
    unnamed x52 -> x14, local copies, waits for them, and re-layouts: 9.68 us -> 4.55 us
    slice x6, local copies, waits for them, and re-layouts: 5.81 us -> 1.65 us  [local(): part = product[:, :, :, place * channels:(place + 1) * channels]]
    ppermute x0 -> x5, starting transfers between devices: none -> 2.53 us  [exchange_sum(): lax.ppermute(value, axis, [(i, i ^ distance) for i in range(count)])]
    ppermute x2, starting transfers between devices: 9.46 us -> 7.13 us  [from_behind(): lax.ppermute(value, axis, [(source, source + steps) for source in range(i...]
  transfers between devices with their start and end apart: 4 -> 8, of which waited for: 3 -> 8; matrix products, arithmetic and copies ran while one was open for 8% -> 11% of each run, Pallas kernels for 0% -> 0%
where the time goes in v1:
time: 136 us
  waiting for transfers between devices  93.1 us (68%)
  between operations  14.3 us (11%)
  starting transfers between devices  9.7 us (7%)
  local copies, waits for them, and re-layouts  8.23 us (6%)
  matrix products  6.09 us (4%)
  other arithmetic  4.23 us (3%)
    ppermute x5, waiting for transfers between devices, exchange_sum(): lax.ppermute(value, axis, [(i, i ^ distance) for i in range(count)])  39.2 us
    all_gather x1, waiting for transfers between devices, local(): gathered = lax.all_gather(cotangent, 'chan', axis=3, tiled=True)  28 us
    ppermute x2, waiting for transfers between devices, from_behind(): lax.ppermute(value, axis, [(source, source + steps) for source in range(i...  25.3 us
    ppermute x2, starting transfers between devices, from_behind(): lax.ppermute(value, axis, [(source, source + steps) for source in range(i...  7.13 us
    unnamed x14, local copies, waits for them, and re-layouts  4.55 us
    dot_general x9, matrix products, local(): jnp.einsum('bxzcy,kc->bxzky', slab, kernel, preferred_element_type=jnp.fl...  3.78 us
    convert_element_type x1, other arithmetic, local(): input_grad = accum.astype(jnp.bfloat16)  3.38 us
  transfers between devices with their start and end apart: 8, of which 8 were waited for; matrix products, arithmetic and copies ran while one was open for 11% of the time, Pallas kernels for 0%

profile of v1, /device:TPU:4, one launch (start us, length us, event | category | flops | bytes accessed | tf_op | source)
XLA Modules:
  0.0 135.7 jit_solution(2542420532690271903)
XLA Ops:
  7.2 0.7 all-gather.2.cloned.1.call-update
  7.9 1.1 fusion.64
  9.0 1.0 fusion.60
  10.0 1.1 fusion.65
  11.1 1.1 fusion.62
  12.7 28.0 %all-gather.2.cloned.1.call-done = bf16[1,2,8,128,512]{4,3,2,1,0:T(8,128)(2,1)} async-done(((bf16[1,2,8,16,512]{4,3,2,1,0:T(8,128)(2,1)}), bf16[1,2,8,128,512]{4,3,2,1,0:T(8,128)(2,1)}) %all-gather.2.cloned.1.call-update) | async-done | bytes 2097168 | tf_op jit(solution)/shard_map/all_gather | solution.py:36
  40.7 1.9 %fusion.68 = (bf16[1,1,8,128,512]{4,3,2,1,0:T(8,128)(2,1)S(1)}, bf16[1,1,8,128,512]{4,3,2,1,0:T(8,128)(2,1)S(1)}) fusion(bf16[1,2,8,128,512]{4,3,2,1,0:T(8,128)(2,1)} %all-gather.2.cloned.1.call-done), kind=kLoop, calls=%fused_computation.97 | loop fusion | bytes 4194304 | tf_op jit(solution)/shard_map/slice | solution.py:49
  42.6 5.2 %collective-permute-start = (bf16[1,1,8,128,512]{4,3,2,1,0:T(8,128)(2,1)S(1)}, bf16[1,1,8,128,512]{4,3,2,1,0:T(8,128)(2,1)S(1)}, u32[]{:S(2)}, u32[]{:S(2)}) collective-permute-start(bf16[1,1,8,128,512]{4,3,2,1,0:T(8,128)(2,1)S(1)} %get-tuple-element.3), channel_id=1, source_target_pairs={{16,0},{32,16},{48,32},{64,48},{80,64},{96,80},{112,96},{128,112},... | collective-permute-start | bytes 3145736 | tf_op jit(solution)/shard_map/ppermute | solution.py:12
  47.8 1.9 %collective-permute-start.1 = (bf16[1,1,8,128,512]{4,3,2,1,0:T(8,128)(2,1)S(1)}, bf16[1,1,8,128,512]{4,3,2,1,0:T(8,128)(2,1)S(1)}, u32[]{:S(2)}, u32[]{:S(2)}) collective-permute-start(bf16[1,1,8,128,512]{4,3,2,1,0:T(8,128)(2,1)S(1)} %get-tuple-element.2), channel_id=1, source_target_pairs={{0,16},{16,32},{32,48},{48,64},{64,80},{80,96},{96,112},{112,128},... | collective-permute-start | bytes 3145736 | tf_op jit(solution)/shard_map/ppermute | solution.py:12
  50.7 0.4 fusion.13
  51.1 0.4 fusion.72
  51.5 0.8 fusion.25
  52.3 18.3 %collective-permute-done = bf16[1,1,8,128,512]{4,3,2,1,0:T(8,128)(2,1)S(1)} collective-permute-done((bf16[1,1,8,128,512]{4,3,2,1,0:T(8,128)(2,1)S(1)}, bf16[1,1,8,128,512]{4,3,2,1,0:T(8,128)(2,1)S(1)}, u32[]{:S(2)}, u32[]{:S(2)}) %collective-permute-start) | collective-permute-done | bytes 1048608 | tf_op jit(solution)/shard_map/ppermute | solution.py:12
  70.6 0.8 fusion.22
  71.3 7.1 %collective-permute-done.1 = bf16[1,1,8,128,512]{4,3,2,1,0:T(8,128)(2,1)S(1)} collective-permute-done((bf16[1,1,8,128,512]{4,3,2,1,0:T(8,128)(2,1)S(1)}, bf16[1,1,8,128,512]{4,3,2,1,0:T(8,128)(2,1)S(1)}, u32[]{:S(2)}, u32[]{:S(2)}) %collective-permute-start.1) | collective-permute-done | bytes 1048608 | tf_op jit(solution)/shard_map/ppermute | solution.py:12
  78.4 0.8 fusion.30
  79.2 2.2 %collective-permute-start.2 = (f32[27,16,128]{2,1,0:T(8,128)S(1)}, f32[27,16,128]{2,1,0:T(8,128)S(1)}, u32[]{:S(2)}, u32[]{:S(2)}) collective-permute-start(f32[27,16,128]{2,1,0:T(8,128)S(1)} %bitcast.157), channel_id=1, source_target_pairs={{0,1},{1,0},{2,3},{3,2},{4,5},{5,4},{6,7},{7,6},{8,9},{9,8},{10,11... | collective-permute-start | bytes 663560 | tf_op jit(solution)/shard_map/ppermute | solution.py:17
  81.4 0.4 convolution_bitcast_fusion.4
  81.8 0.4 convolution_bitcast_fusion.5
  82.2 0.4 fusion.69
  82.6 0.4 convolution_bitcast_fusion.1
  83.1 0.4 convolution_bitcast_fusion.2
  83.5 2.5 %collective-permute-done.2 = f32[27,16,128]{2,1,0:T(8,128)S(1)} collective-permute-done((f32[27,16,128]{2,1,0:T(8,128)S(1)}, f32[27,16,128]{2,1,0:T(8,128)S(1)}, u32[]{:S(2)}, u32[]{:S(2)}) %collective-permute-start.2) | collective-permute-done | bytes 221216 | tf_op jit(solution)/shard_map/ppermute | solution.py:17
  86.1 0.4 fusion.75
  86.5 0.4 convolution_bitcast_fusion.3
  87.0 5.1 %collective-permute-done.3 = f32[27,16,128]{2,1,0:T(8,128)S(1)} collective-permute-done((f32[27,16,128]{2,1,0:T(8,128)S(1)}, f32[27,16,128]{2,1,0:T(8,128)S(1)}, u32[]{:S(2)}, u32[]{:S(2)}) %collective-permute-start.3) | collective-permute-done | bytes 221216 | tf_op jit(solution)/shard_map/ppermute | solution.py:17
  92.3 0.4 convolution_bitcast_fusion
  92.7 6.9 %collective-permute-done.4 = f32[27,16,128]{2,1,0:T(8,128)S(1)} collective-permute-done((f32[27,16,128]{2,1,0:T(8,128)S(1)}, f32[27,16,128]{2,1,0:T(8,128)S(1)}, u32[]{:S(2)}, u32[]{:S(2)}) %collective-permute-start.4) | collective-permute-done | bytes 221216 | tf_op jit(solution)/shard_map/ppermute | solution.py:17
  99.8 18.3 %collective-permute-done.5 = f32[27,16,128]{2,1,0:T(8,128)S(1)} collective-permute-done((f32[27,16,128]{2,1,0:T(8,128)S(1)}, f32[27,16,128]{2,1,0:T(8,128)S(1)}, u32[]{:S(2)}, u32[]{:S(2)}) %collective-permute-start.5) | collective-permute-done | bytes 221216 | tf_op jit(solution)/shard_map/ppermute | solution.py:17
  118.3 3.4 %fusion.59 = bf16[1,2,8,16,512]{4,3,2,1,0:T(8,128)(2,1)} fusion(f32[1,2,8,16,512]{4,3,2,1,0:T(8,128)S(1)} %get-tuple-element.26, f32[1,2,8,16,512]{4,3,2,1,0:T(8,128)S(1)} %get-tuple-element.27, f32[1,2,8,16,512]{4,3,2,1,0:T(8,128)S(1)} %get-tuple-element.25, f32[1,2,8,16,512]{4,3,2,1,0:T(8,128)S(1)} %get-tuple-element.41, ...), kind=kLoop, calls=%fused_computation.77 | loop fusion | flops 3538944 | bytes 14417920 | tf_op jit(solution)/shard_map/convert_element_type | solution.py:64
  121.7 6.4 %collective-permute-done.6 = f32[27,16,128]{2,1,0:T(8,128)S(1)} collective-permute-done((f32[27,16,128]{2,1,0:T(8,128)S(1)}, f32[27,16,128]{2,1,0:T(8,128)S(1)}, u32[]{:S(2)}, u32[]{:S(2)}) %collective-permute-start.6) | collective-permute-done | bytes 221216 | tf_op jit(solution)/shard_map/ppermute | solution.py:17
  128.1 0.7 add_multiply_fusion
  (27 shorter events, 2.2 us)
Async XLA Ops:
  7.2 5.0 %copy-start.1 = (bf16[1,2,8,16,512]{4,3,2,1,0:T(8,128)(2,1)S(1)}, bf16[1,2,8,16,512]{4,3,2,1,0:T(8,128)(2,1)}, u32[]{:S(2)}) copy-start(bf16[1,2,8,16,512]{4,3,2,1,0:T(8,128)(2,1)} %param.3) | copy-start | bytes 786436
  7.2 33.5 %all-gather.2.cloned.1.call-start = ((), (), s32[]{:S(2)}) async-start(), calls=%async_computation | async-start | bytes 2359296 | tf_op jit(solution)/shard_map/all_gather | solution.py:36
  9.0 3.7 %copy-start.2 = (bf16[27,16,128]{2,1,0:T(8,128)(2,1)S(1)}, bf16[27,16,128]{2,1,0:T(8,128)(2,1)}, u32[]{:S(2)}) copy-start(bf16[27,16,128]{2,1,0:T(8,128)(2,1)} %param.5) | copy-start | bytes 331780
  40.7 9.0 %copy-start = (bf16[1,2,8,128,512]{4,3,2,1,0:T(8,128)(2,1)S(1)}, bf16[1,2,8,128,512]{4,3,2,1,0:T(8,128)(2,1)}, u32[]{:S(2)}) copy-start(bf16[1,2,8,128,512]{4,3,2,1,0:T(8,128)(2,1)} %all-gather.2.cloned.1.call-done) | copy-start | bytes 6291460
  42.6 28.0 %collective-permute-start = (bf16[1,1,8,128,512]{4,3,2,1,0:T(8,128)(2,1)S(1)}, bf16[1,1,8,128,512]{4,3,2,1,0:T(8,128)(2,1)S(1)}, u32[]{:S(2)}, u32[]{:S(2)}) collective-permute-start(bf16[1,1,8,128,512]{4,3,2,1,0:T(8,128)(2,1)S(1)} %get-tuple-element.3), channel_id=1, source_target_pairs={{16,0},{32,16},{48,32},{64,48},{80,64},{96,80},{112,96},{128,112},... | collective-permute-start | bytes 3145736 | tf_op jit(solution)/shard_map/ppermute | solution.py:12
  47.8 30.6 %collective-permute-start.1 = (bf16[1,1,8,128,512]{4,3,2,1,0:T(8,128)(2,1)S(1)}, bf16[1,1,8,128,512]{4,3,2,1,0:T(8,128)(2,1)S(1)}, u32[]{:S(2)}, u32[]{:S(2)}) collective-permute-start(bf16[1,1,8,128,512]{4,3,2,1,0:T(8,128)(2,1)S(1)} %get-tuple-element.2), channel_id=1, source_target_pairs={{0,16},{16,32},{32,48},{48,64},{64,80},{80,96},{96,112},{112,128},... | collective-permute-start | bytes 3145736 | tf_op jit(solution)/shard_map/ppermute | solution.py:12
  79.2 6.8 %collective-permute-start.2 = (f32[27,16,128]{2,1,0:T(8,128)S(1)}, f32[27,16,128]{2,1,0:T(8,128)S(1)}, u32[]{:S(2)}, u32[]{:S(2)}) collective-permute-start(f32[27,16,128]{2,1,0:T(8,128)S(1)} %bitcast.157), channel_id=1, source_target_pairs={{0,1},{1,0},{2,3},{3,2},{4,5},{5,4},{6,7},{7,6},{8,9},{9,8},{10,11... | collective-permute-start | bytes 663560 | tf_op jit(solution)/shard_map/ppermute | solution.py:17
  86.0 6.0 %collective-permute-start.3 = (f32[27,16,128]{2,1,0:T(8,128)S(1)}, f32[27,16,128]{2,1,0:T(8,128)S(1)}, u32[]{:S(2)}, u32[]{:S(2)}) collective-permute-start(f32[27,16,128]{2,1,0:T(8,128)S(1)} %add.183), channel_id=1, source_target_pairs={{0,16},{16,0},{32,48},{48,32},{64,80},{80,64},{96,112},{112,96},{1... | collective-permute-start | bytes 663560 | tf_op jit(solution)/shard_map/ppermute | solution.py:17
  92.1 7.5 %collective-permute-start.4 = (f32[27,16,128]{2,1,0:T(8,128)S(1)}, f32[27,16,128]{2,1,0:T(8,128)S(1)}, u32[]{:S(2)}, u32[]{:S(2)}) collective-permute-start(f32[27,16,128]{2,1,0:T(8,128)S(1)} %add.184), channel_id=1, source_target_pairs={{0,128},{16,144},{32,160},{48,176},{64,192},{80,208},{96,224},{112... | collective-permute-start | bytes 663560 | tf_op jit(solution)/shard_map/ppermute | solution.py:17
  99.6 18.6 %collective-permute-start.5 = (f32[27,16,128]{2,1,0:T(8,128)S(1)}, f32[27,16,128]{2,1,0:T(8,128)S(1)}, u32[]{:S(2)}, u32[]{:S(2)}) collective-permute-start(f32[27,16,128]{2,1,0:T(8,128)S(1)} %add.185), channel_id=1, source_target_pairs={{0,32},{16,48},{32,0},{48,16},{64,96},{80,112},{96,64},{112,80},{1... | collective-permute-start | bytes 663560 | tf_op jit(solution)/shard_map/ppermute | solution.py:17
  118.2 9.9 %collective-permute-start.6 = (f32[27,16,128]{2,1,0:T(8,128)S(1)}, f32[27,16,128]{2,1,0:T(8,128)S(1)}, u32[]{:S(2)}, u32[]{:S(2)}) collective-permute-start(f32[27,16,128]{2,1,0:T(8,128)S(1)} %add.186), channel_id=1, source_target_pairs={{0,64},{16,80},{32,96},{48,112},{64,0},{80,16},{96,32},{112,48},{1... | collective-permute-start | bytes 663560 | tf_op jit(solution)/shard_map/ppermute | solution.py:17
Sparse Core Ops, SparseCore 0:
  9.8 30.7 all-gather.1

commit v2 on v1

--- a/solution.py
+++ b/solution.py
@@ -33,15 +33,33 @@
 def local(inputs, cotangent, weight):
     samples, planes, depth, channels, width = inputs.shape
     outputs = weight.shape[2]
+    inputs_ext = jnp.concatenate(
+        [from_behind(inputs[:, -1:], "space", 1), inputs, from_behind(inputs[:, :1], "space", -1)],
+        axis=1,
+    )
+    cot_halo = jnp.concatenate(
+        [from_behind(cotangent[:, -1:], "space", 1), from_behind(cotangent[:, :1], "space", -1)],
+        axis=1,
+    )
     gathered = lax.all_gather(cotangent, "chan", axis=3, tiled=True)
-    lower_plane = from_behind(gathered[:, -1:], "space", 1)
-    upper_plane = from_behind(gathered[:, :1], "space", -1)
     stacked = jnp.concatenate(
-        [shift_cells(inputs, -step_z, -step_y) for step_z in (-1, 0, 1) for step_y in (-1, 0, 1)],
+        [shift_cells(inputs_ext, -step_z, -step_y) for step_z in (-1, 0, 1) for step_y in (-1, 0, 1)],
         axis=3,
     )
+    groups = []
+    for step_x in (-1, 0, 1):
+        source = stacked[:, 1 + step_x : 1 + step_x + planes]
+        groups.append(
+            jnp.einsum("bxzky,bxzcy->kc", source, gathered, preferred_element_type=jnp.float32)
+        )
+    local_grad = jnp.concatenate(groups, axis=0).reshape(27, channels, outputs)
+    count = samples * lax.axis_size("dp") * planes * lax.axis_size("space") * depth * width
+    scale = 1.0 / math.sqrt(count)
+    weight_grad = butterfly_sum(local_grad) * scale
+
+    halo = lax.all_gather(cot_halo, "chan", axis=3, tiled=True)
+    lower_plane, upper_plane = halo[:, :1], halo[:, 1:]
     accum = jnp.zeros(inputs.shape, jnp.float32)
-    groups = []
     for step_x in (-1, 0, 1):
         if step_x == 1:
             slab = jnp.concatenate([lower_plane, gathered[:, : planes - 1]], axis=1)
@@ -50,9 +68,6 @@
         else:
             slab = gathered
         first = 9 * (step_x + 1)
-        groups.append(
-            jnp.einsum("bxzky,bxzcy->kc", stacked, slab, preferred_element_type=jnp.float32)
-        )
         for step_y in (-1, 0, 1):
             kernel = weight[first + step_y + 1 : first + 9 : 3].reshape(3 * channels, outputs)
             product = jnp.einsum(
@@ -62,10 +77,6 @@
                 part = product[:, :, :, place * channels : (place + 1) * channels]
                 accum = accum + shift_cells(part, step_z, step_y)
     input_grad = accum.astype(jnp.bfloat16)
-    local_grad = jnp.concatenate(groups, axis=0).reshape(27, channels, outputs)
-    count = samples * lax.axis_size("dp") * planes * lax.axis_size("space") * depth * width
-    scale = 1.0 / math.sqrt(count)
-    weight_grad = butterfly_sum(local_grad) * scale
     return (input_grad, weight_grad)
 
 

time: 136 us -> 128 us (0.941)
  waiting for transfers between devices: 93.1 us -> 42.8 us
  starting transfers between devices: 9.7 us -> 32.1 us
  local copies, waits for them, and re-layouts: 8.23 us -> 19.8 us
  matrix products: 6.09 us -> 11.9 us
  other arithmetic: 4.23 us -> 6.83 us
    all_gather x1, waiting for transfers between devices: 28 us -> 0.01 us  [local(): gathered = lax.all_gather(cotangent, 'chan', axis=3, tiled=True)]
    ppermute x2 -> x4, waiting for transfers between devices: 25.3 us -> 0.6 us  [from_behind(): lax.ppermute(value, axis, [(source, source + steps) for source in range(i...]
    all_gather x0 -> x1, waiting for transfers between devices: none -> 14.5 us  [local(): halo = lax.all_gather(cot_halo, 'chan', axis=3, tiled=True)]
    ppermute x5, waiting for transfers between devices: 39.2 us -> 27 us  [exchange_sum(): lax.ppermute(value, axis, [(i, i ^ distance) for i in range(count)])]
    ppermute x2 -> x4, starting transfers between devices: 7.13 us -> 19.1 us  [from_behind(): lax.ppermute(value, axis, [(source, source + steps) for source in range(i...]
    ppermute x5, starting transfers between devices: 2.53 us -> 13 us  [exchange_sum(): lax.ppermute(value, axis, [(i, i ^ distance) for i in range(count)])]
    unnamed x14 -> x30, local copies, waits for them, and re-layouts: 4.55 us -> 10.3 us
    dot_general x3, matrix products: 2.31 us -> 8.07 us  [local(): jnp.einsum('bxzky,bxzcy->kc', source, gathered, preferred_element_type=jn...]
  transfers between devices with their start and end apart: 8 -> 11, of which waited for: 8 -> 6; matrix products, arithmetic and copies ran while one was open for 11% -> 29% of each run, Pallas kernels for 0% -> 0%
where the time goes in v2:
time: 128 us
  waiting for transfers between devices  42.8 us (33%)
  starting transfers between devices  32.1 us (25%)
  local copies, waits for them, and re-layouts  19.8 us (15%)
  between operations  14.3 us (11%)
  matrix products  11.9 us (9%)
  other arithmetic  6.83 us (5%)
    ppermute x5, waiting for transfers between devices, exchange_sum(): lax.ppermute(value, axis, [(i, i ^ distance) for i in range(count)])  27 us
    ppermute x4, starting transfers between devices, from_behind(): lax.ppermute(value, axis, [(source, source + steps) for source in range(i...  19.1 us
    all_gather x1, waiting for transfers between devices, local(): halo = lax.all_gather(cot_halo, 'chan', axis=3, tiled=True)  14.5 us
    ppermute x5, starting transfers between devices, exchange_sum(): lax.ppermute(value, axis, [(i, i ^ distance) for i in range(count)])  13 us
    unnamed x30, local copies, waits for them, and re-layouts  10.3 us
    dot_general x3, matrix products, local(): jnp.einsum('bxzky,bxzcy->kc', source, gathered, preferred_element_type=jn...  8.07 us
    convert_element_type x1, other arithmetic, local(): input_grad = accum.astype(jnp.bfloat16)  4.32 us
    dot_general x9, matrix products, local(): jnp.einsum('bxzcy,kc->bxzky', slab, kernel, preferred_element_type=jnp.fl...  3.79 us
  transfers between devices with their start and end apart: 11, of which 6 were waited for; matrix products, arithmetic and copies ran while one was open for 29% of the time, Pallas kernels for 0%

profile of v2, /device:TPU:4, one launch (start us, length us, event | category | flops | bytes accessed | tf_op | source)
XLA Modules:
  0.0 127.8 jit_solution(1748607071832036304)
XLA Ops:
  7.9 1.0 fusion.82
  8.9 3.8 %collective-permute-start.2 = (bf16[1,1,8,16,512]{4,3,2,1,0:T(8,128)(2,1)S(1)}, bf16[1,1,8,16,512]{4,3,2,1,0:T(8,128)(2,1)S(1)}, u32[]{:S(2)}, u32[]{:S(2)}) collective-permute-start(bf16[1,1,8,16,512]{4,3,2,1,0:T(8,128)(2,1)S(1)} %get-tuple-element.31), channel_id=1, source_target_pairs={{0,16},{16,32},{32,48},{48,64},{64,80},{80,96},{96,112},{112,128},... | collective-permute-start | bytes 393224 | tf_op jit(solution)/shard_map/ppermute | solution.py:12
  12.8 5.8 %collective-permute-start.3 = (bf16[1,1,8,16,512]{4,3,2,1,0:T(8,128)(2,1)S(1)}, bf16[1,1,8,16,512]{4,3,2,1,0:T(8,128)(2,1)S(1)}, u32[]{:S(2)}, u32[]{:S(2)}) collective-permute-start(bf16[1,1,8,16,512]{4,3,2,1,0:T(8,128)(2,1)S(1)} %get-tuple-element.30), channel_id=1, source_target_pairs={{16,0},{32,16},{48,32},{64,48},{80,64},{96,80},{112,96},{128,112},... | collective-permute-start | bytes 393224 | tf_op jit(solution)/shard_map/ppermute | solution.py:12
  18.6 1.0 fusion.83
  19.6 1.9 %collective-permute-start = (bf16[1,1,8,16,512]{4,3,2,1,0:T(8,128)(2,1)S(1)}, bf16[1,1,8,16,512]{4,3,2,1,0:T(8,128)(2,1)S(1)}, u32[]{:S(2)}, u32[]{:S(2)}) collective-permute-start(bf16[1,1,8,16,512]{4,3,2,1,0:T(8,128)(2,1)S(1)} %get-tuple-element.32), channel_id=1, source_target_pairs={{0,16},{16,32},{32,48},{48,64},{64,80},{80,96},{96,112},{112,128},... | collective-permute-start | bytes 393224 | tf_op jit(solution)/shard_map/ppermute | solution.py:12
  21.5 7.5 %collective-permute-start.1 = (bf16[1,1,8,16,512]{4,3,2,1,0:T(8,128)(2,1)S(1)}, bf16[1,1,8,16,512]{4,3,2,1,0:T(8,128)(2,1)S(1)}, u32[]{:S(2)}, u32[]{:S(2)}) collective-permute-start(bf16[1,1,8,16,512]{4,3,2,1,0:T(8,128)(2,1)S(1)} %get-tuple-element.33), channel_id=1, source_target_pairs={{16,0},{32,16},{48,32},{64,48},{80,64},{96,80},{112,96},{128,112},... | collective-permute-start | bytes 393224 | tf_op jit(solution)/shard_map/ppermute | solution.py:12
  29.9 1.0 constant_dynamic-update-slice_fusion.1
  32.3 1.0 fusion.60
  33.3 0.9 fusion.30
  34.2 1.1 fusion.61
  35.3 1.2 fusion.56
  38.5 1.1 fusion.57
  39.7 1.1 fusion.62
  40.7 0.9 fusion.31
  41.6 1.0 fusion.63
  42.6 3.2 %fusion.21 = f32[144,128]{1,0:T(8,128)S(1)} fusion(bf16[1,2,8,128,512]{4,3,2,1,0:T(8,128)(2,1)} %all-gather.3.cloned.1.call-done, bf16[1,4,8,144,512]{4,3,2,1,0:T(8,128)(2,1)} %fusion.63), kind=kOutput, calls=%fused_computation.26 | convolution fusion | flops 301989888 | bytes 4530176 | tf_op jit(solution)/shard_map/bxzky,bxzcy->kc/dot_general | solution.py:53
  45.9 2.4 %fusion.24 = f32[144,128]{1,0:T(8,128)S(1)} fusion(bf16[1,2,8,128,512]{4,3,2,1,0:T(8,128)(2,1)S(1)} %copy-done, bf16[1,4,8,144,512]{4,3,2,1,0:T(8,128)(2,1)} %fusion.63), kind=kOutput, calls=%fused_computation.27 | convolution fusion | flops 301989888 | bytes 4530176 | tf_op jit(solution)/shard_map/bxzky,bxzcy->kc/dot_general | solution.py:53
  48.3 2.4 %fusion.27 = f32[144,128]{1,0:T(8,128)S(1)} fusion(bf16[1,2,8,128,512]{4,3,2,1,0:T(8,128)(2,1)S(1)} %copy-done, bf16[1,4,8,144,512]{4,3,2,1,0:T(8,128)(2,1)} %fusion.63), kind=kOutput, calls=%fused_computation.28 | convolution fusion | flops 301989888 | bytes 4530176 | tf_op jit(solution)/shard_map/bxzky,bxzcy->kc/dot_general | solution.py:53
  50.8 2.2 %collective-permute-start.4 = (f32[27,16,128]{2,1,0:T(8,128)S(1)}, f32[27,16,128]{2,1,0:T(8,128)}, u32[]{:S(2)}, u32[]{:S(2)}) collective-permute-start(f32[27,16,128]{2,1,0:T(8,128)S(1)} %bitcast.165), channel_id=1, source_target_pairs={{0,1},{1,0},{2,3},{3,2},{4,5},{5,4},{6,7},{7,6},{8,9},{9,8},{10,11... | collective-permute-start | bytes 663560 | tf_op jit(solution)/shard_map/ppermute | solution.py:17
  54.2 1.2 fusion.78
  55.6 1.2 fusion.76
  56.8 14.5 %all-gather.5.cloned.1.call-done = bf16[1,2,8,128,512]{4,3,2,1,0:T(8,128)(2,1)} async-done(((bf16[1,2,8,16,512]{4,3,2,1,0:T(8,128)(2,1)}), bf16[1,2,8,128,512]{4,3,2,1,0:T(8,128)(2,1)}) %all-gather.5.cloned.1.call-update) | async-done | bytes 2097168 | tf_op jit(solution)/shard_map/all_gather | solution.py:60
  71.3 1.7 %fusion.72 = (bf16[1,1,8,128,512]{4,3,2,1,0:T(8,128)(2,1)S(1)}, bf16[1,1,8,128,512]{4,3,2,1,0:T(8,128)(2,1)S(1)}) fusion(bf16[1,2,8,128,512]{4,3,2,1,0:T(8,128)(2,1)} %all-gather.5.cloned.1.call-done), kind=kLoop, calls=%fused_computation.112 | loop fusion | bytes 4194304 | tf_op jit(solution)/shard_map/slice | solution.py:61
  75.4 1.0 add.183
  76.3 1.6 %collective-permute-start.5 = (f32[27,16,128]{2,1,0:T(8,128)S(1)}, f32[27,16,128]{2,1,0:T(8,128)S(1)}, u32[]{:S(2)}, u32[]{:S(2)}) collective-permute-start(f32[27,16,128]{2,1,0:T(8,128)S(1)} %add.183), channel_id=1, source_target_pairs={{0,16},{16,0},{32,48},{48,32},{64,80},{80,64},{96,112},{112,96},{1... | collective-permute-start | bytes 663560 | tf_op jit(solution)/shard_map/ppermute | solution.py:17
  78.3 5.6 %collective-permute-done.5 = f32[27,16,128]{2,1,0:T(8,128)S(1)} collective-permute-done((f32[27,16,128]{2,1,0:T(8,128)S(1)}, f32[27,16,128]{2,1,0:T(8,128)S(1)}, u32[]{:S(2)}, u32[]{:S(2)}) %collective-permute-start.5) | collective-permute-done | bytes 221216 | tf_op jit(solution)/shard_map/ppermute | solution.py:17
  85.5 6.8 %collective-permute-done.6 = f32[27,16,128]{2,1,0:T(8,128)S(1)} collective-permute-done((f32[27,16,128]{2,1,0:T(8,128)S(1)}, f32[27,16,128]{2,1,0:T(8,128)S(1)}, u32[]{:S(2)}, u32[]{:S(2)}) %collective-permute-start.6) | collective-permute-done | bytes 221216 | tf_op jit(solution)/shard_map/ppermute | solution.py:17
  92.4 2.6 %collective-permute-start.7 = (f32[27,16,128]{2,1,0:T(8,128)S(1)}, f32[27,16,128]{2,1,0:T(8,128)S(1)}, u32[]{:S(2)}, u32[]{:S(2)}) collective-permute-start(f32[27,16,128]{2,1,0:T(8,128)S(1)} %add.185), channel_id=1, source_target_pairs={{0,32},{16,48},{32,0},{48,16},{64,96},{80,112},{96,64},{112,80},{1... | collective-permute-start | bytes 663560 | tf_op jit(solution)/shard_map/ppermute | solution.py:17
  95.4 8.6 %collective-permute-done.7 = f32[27,16,128]{2,1,0:T(8,128)S(1)} collective-permute-done((f32[27,16,128]{2,1,0:T(8,128)S(1)}, f32[27,16,128]{2,1,0:T(8,128)S(1)}, u32[]{:S(2)}, u32[]{:S(2)}) %collective-permute-start.7) | collective-permute-done | bytes 221216 | tf_op jit(solution)/shard_map/ppermute | solution.py:17
  104.0 5.9 %collective-permute-start.8 = (f32[27,16,128]{2,1,0:T(8,128)S(1)}, f32[27,16,128]{2,1,0:T(8,128)S(1)}, u32[]{:S(2)}, u32[]{:S(2)}) collective-permute-start(f32[27,16,128]{2,1,0:T(8,128)S(1)} %add.186), channel_id=1, source_target_pairs={{0,64},{16,80},{32,96},{48,112},{64,0},{80,16},{96,32},{112,48},{1... | collective-permute-start | bytes 663560 | tf_op jit(solution)/shard_map/ppermute | solution.py:17
  109.9 4.3 %fusion.64 = bf16[1,2,8,16,512]{4,3,2,1,0:T(8,128)(2,1)} fusion(f32[1,2,8,16,512]{4,3,2,1,0:T(8,128)S(1)} %get-tuple-element.51, f32[1,2,8,16,512]{4,3,2,1,0:T(8,128)S(1)} %get-tuple-element.50, f32[1,2,8,16,512]{4,3,2,1,0:T(8,128)S(1)} %get-tuple-element.52, f32[1,2,8,16,512]{4,3,2,1,0:T(8,128)S(1)} %get-tuple-element.26, ...), kind=kLoop, calls=%fused_computation.95 | loop fusion | flops 3538944 | bytes 14417920 | tf_op jit(solution)/shard_map/convert_element_type | solution.py:79
  114.2 6.0 %collective-permute-done.8 = f32[27,16,128]{2,1,0:T(8,128)S(1)} collective-permute-done((f32[27,16,128]{2,1,0:T(8,128)S(1)}, f32[27,16,128]{2,1,0:T(8,128)S(1)}, u32[]{:S(2)}, u32[]{:S(2)}) %collective-permute-start.8) | collective-permute-done | bytes 221216 | tf_op jit(solution)/shard_map/ppermute | solution.py:17
  (54 shorter events, 11.8 us)
Async XLA Ops:
  7.2 35.5 %all-gather.3.cloned.1.call-start = ((), (), s32[]{:S(2)}) async-start(), calls=%async_computation | async-start | bytes 2359296 | tf_op jit(solution)/shard_map/all_gather | solution.py:44
  7.9 63.4 %all-gather.5.cloned.1.call-start = ((), (), s32[]{:S(2)}) async-start(), calls=%async_computation.1 | async-start | bytes 2359296 | tf_op jit(solution)/shard_map/all_gather | solution.py:60
  8.9 21.0 %collective-permute-start.2 = (bf16[1,1,8,16,512]{4,3,2,1,0:T(8,128)(2,1)S(1)}, bf16[1,1,8,16,512]{4,3,2,1,0:T(8,128)(2,1)S(1)}, u32[]{:S(2)}, u32[]{:S(2)}) collective-permute-start(bf16[1,1,8,16,512]{4,3,2,1,0:T(8,128)(2,1)S(1)} %get-tuple-element.31), channel_id=1, source_target_pairs={{0,16},{16,32},{32,48},{48,64},{64,80},{80,96},{96,112},{112,128},... | collective-permute-start | bytes 393224 | tf_op jit(solution)/shard_map/ppermute | solution.py:12
  12.8 18.1 %collective-permute-start.3 = (bf16[1,1,8,16,512]{4,3,2,1,0:T(8,128)(2,1)S(1)}, bf16[1,1,8,16,512]{4,3,2,1,0:T(8,128)(2,1)S(1)}, u32[]{:S(2)}, u32[]{:S(2)}) collective-permute-start(bf16[1,1,8,16,512]{4,3,2,1,0:T(8,128)(2,1)S(1)} %get-tuple-element.30), channel_id=1, source_target_pairs={{16,0},{32,16},{48,32},{64,48},{80,64},{96,80},{112,96},{128,112},... | collective-permute-start | bytes 393224 | tf_op jit(solution)/shard_map/ppermute | solution.py:12
  19.6 11.4 %collective-permute-start = (bf16[1,1,8,16,512]{4,3,2,1,0:T(8,128)(2,1)S(1)}, bf16[1,1,8,16,512]{4,3,2,1,0:T(8,128)(2,1)S(1)}, u32[]{:S(2)}, u32[]{:S(2)}) collective-permute-start(bf16[1,1,8,16,512]{4,3,2,1,0:T(8,128)(2,1)S(1)} %get-tuple-element.32), channel_id=1, source_target_pairs={{0,16},{16,32},{32,48},{48,64},{64,80},{80,96},{96,112},{112,128},... | collective-permute-start | bytes 393224 | tf_op jit(solution)/shard_map/ppermute | solution.py:12
  21.5 10.0 %collective-permute-start.1 = (bf16[1,1,8,16,512]{4,3,2,1,0:T(8,128)(2,1)S(1)}, bf16[1,1,8,16,512]{4,3,2,1,0:T(8,128)(2,1)S(1)}, u32[]{:S(2)}, u32[]{:S(2)}) collective-permute-start(bf16[1,1,8,16,512]{4,3,2,1,0:T(8,128)(2,1)S(1)} %get-tuple-element.33), channel_id=1, source_target_pairs={{16,0},{32,16},{48,32},{64,48},{80,64},{96,80},{112,96},{128,112},... | collective-permute-start | bytes 393224 | tf_op jit(solution)/shard_map/ppermute | solution.py:12
  33.3 3.8 %copy-start.2 = (bf16[1,2,8,16,512]{4,3,2,1,0:T(8,128)(2,1)S(1)}, bf16[1,2,8,16,512]{4,3,2,1,0:T(8,128)(2,1)}, u32[]{:S(2)}) copy-start(bf16[1,2,8,16,512]{4,3,2,1,0:T(8,128)(2,1)} %param.3) | copy-start | bytes 786436
  42.6 3.2 %copy-start = (bf16[1,2,8,128,512]{4,3,2,1,0:T(8,128)(2,1)S(1)}, bf16[1,2,8,128,512]{4,3,2,1,0:T(8,128)(2,1)}, u32[]{:S(2)}) copy-start(bf16[1,2,8,128,512]{4,3,2,1,0:T(8,128)(2,1)} %all-gather.3.cloned.1.call-done) | copy-start | bytes 6291460
  50.8 24.6 %collective-permute-start.4 = (f32[27,16,128]{2,1,0:T(8,128)S(1)}, f32[27,16,128]{2,1,0:T(8,128)}, u32[]{:S(2)}, u32[]{:S(2)}) collective-permute-start(f32[27,16,128]{2,1,0:T(8,128)S(1)} %bitcast.165), channel_id=1, source_target_pairs={{0,1},{1,0},{2,3},{3,2},{4,5},{5,4},{6,7},{7,6},{8,9},{9,8},{10,11... | collective-permute-start | bytes 663560 | tf_op jit(solution)/shard_map/ppermute | solution.py:17
  53.4 2.3 %copy-start.1 = (f32[1,2,8,48,512]{4,3,2,1,0:T(8,128)}, f32[1,2,8,48,512]{4,3,2,1,0:T(8,128)S(1)}, u32[]{:S(2)}) copy-start(f32[1,2,8,48,512]{4,3,2,1,0:T(8,128)S(1)} %fusion.15) | copy-start | bytes 4718596
  76.3 7.6 %collective-permute-start.5 = (f32[27,16,128]{2,1,0:T(8,128)S(1)}, f32[27,16,128]{2,1,0:T(8,128)S(1)}, u32[]{:S(2)}, u32[]{:S(2)}) collective-permute-start(f32[27,16,128]{2,1,0:T(8,128)S(1)} %add.183), channel_id=1, source_target_pairs={{0,16},{16,0},{32,48},{48,32},{64,80},{80,64},{96,112},{112,96},{1... | collective-permute-start | bytes 663560 | tf_op jit(solution)/shard_map/ppermute | solution.py:17
  84.0 8.3 %collective-permute-start.6 = (f32[27,16,128]{2,1,0:T(8,128)S(1)}, f32[27,16,128]{2,1,0:T(8,128)S(1)}, u32[]{:S(2)}, u32[]{:S(2)}) collective-permute-start(f32[27,16,128]{2,1,0:T(8,128)S(1)} %add.184), channel_id=1, source_target_pairs={{0,128},{16,144},{32,160},{48,176},{64,192},{80,208},{96,224},{112... | collective-permute-start | bytes 663560 | tf_op jit(solution)/shard_map/ppermute | solution.py:17
  92.3 17.5 %copy-start.3 = (f32[1,2,8,16,512]{4,3,2,1,0:T(8,128)S(1)}, f32[1,2,8,16,512]{4,3,2,1,0:T(8,128)}, u32[]{:S(2)}) copy-start(f32[1,2,8,16,512]{4,3,2,1,0:T(8,128)} %get-tuple-element.16) | copy-start | bytes 1572868
  92.3 17.5 %copy-start.4 = (f32[1,2,8,16,512]{4,3,2,1,0:T(8,128)S(1)}, f32[1,2,8,16,512]{4,3,2,1,0:T(8,128)}, u32[]{:S(2)}) copy-start(f32[1,2,8,16,512]{4,3,2,1,0:T(8,128)} %get-tuple-element.48) | copy-start | bytes 1572868
  92.3 17.5 %copy-start.5 = (f32[1,2,8,16,512]{4,3,2,1,0:T(8,128)S(1)}, f32[1,2,8,16,512]{4,3,2,1,0:T(8,128)}, u32[]{:S(2)}) copy-start(f32[1,2,8,16,512]{4,3,2,1,0:T(8,128)} %get-tuple-element.49) | copy-start | bytes 1572868
  92.4 17.5 %copy-start.6 = (f32[1,2,8,16,512]{4,3,2,1,0:T(8,128)S(1)}, f32[1,2,8,16,512]{4,3,2,1,0:T(8,128)}, u32[]{:S(2)}) copy-start(f32[1,2,8,16,512]{4,3,2,1,0:T(8,128)} %get-tuple-element.19) | copy-start | bytes 1572868
  92.4 17.5 %copy-start.7 = (f32[1,2,8,16,512]{4,3,2,1,0:T(8,128)S(1)}, f32[1,2,8,16,512]{4,3,2,1,0:T(8,128)}, u32[]{:S(2)}) copy-start(f32[1,2,8,16,512]{4,3,2,1,0:T(8,128)} %get-tuple-element.20) | copy-start | bytes 1572868
  92.4 17.5 %copy-start.8 = (f32[1,2,8,16,512]{4,3,2,1,0:T(8,128)S(1)}, f32[1,2,8,16,512]{4,3,2,1,0:T(8,128)}, u32[]{:S(2)}) copy-start(f32[1,2,8,16,512]{4,3,2,1,0:T(8,128)} %get-tuple-element.21) | copy-start | bytes 1572868
  92.4 11.6 %collective-permute-start.7 = (f32[27,16,128]{2,1,0:T(8,128)S(1)}, f32[27,16,128]{2,1,0:T(8,128)S(1)}, u32[]{:S(2)}, u32[]{:S(2)}) collective-permute-start(f32[27,16,128]{2,1,0:T(8,128)S(1)} %add.185), channel_id=1, source_target_pairs={{0,32},{16,48},{32,0},{48,16},{64,96},{80,112},{96,64},{112,80},{1... | collective-permute-start | bytes 663560 | tf_op jit(solution)/shard_map/ppermute | solution.py:17
  104.0 16.2 %collective-permute-start.8 = (f32[27,16,128]{2,1,0:T(8,128)S(1)}, f32[27,16,128]{2,1,0:T(8,128)S(1)}, u32[]{:S(2)}, u32[]{:S(2)}) collective-permute-start(f32[27,16,128]{2,1,0:T(8,128)S(1)} %add.186), channel_id=1, source_target_pairs={{0,64},{16,80},{32,96},{48,112},{64,0},{80,16},{96,32},{112,48},{1... | collective-permute-start | bytes 663560 | tf_op jit(solution)/shard_map/ppermute | solution.py:17
Sparse Core Ops, SparseCore 0:
  9.8 30.7 all-gather.2
  43.1 28.2 all-gather.4

commit v3 on v2

--- a/solution.py
+++ b/solution.py
@@ -37,10 +37,6 @@
         [from_behind(inputs[:, -1:], "space", 1), inputs, from_behind(inputs[:, :1], "space", -1)],
         axis=1,
     )
-    cot_halo = jnp.concatenate(
-        [from_behind(cotangent[:, -1:], "space", 1), from_behind(cotangent[:, :1], "space", -1)],
-        axis=1,
-    )
     gathered = lax.all_gather(cotangent, "chan", axis=3, tiled=True)
     stacked = jnp.concatenate(
         [shift_cells(inputs_ext, -step_z, -step_y) for step_z in (-1, 0, 1) for step_y in (-1, 0, 1)],
@@ -57,25 +53,26 @@
     scale = 1.0 / math.sqrt(count)
     weight_grad = butterfly_sum(local_grad) * scale
 
-    halo = lax.all_gather(cot_halo, "chan", axis=3, tiled=True)
-    lower_plane, upper_plane = halo[:, :1], halo[:, 1:]
-    accum = jnp.zeros(inputs.shape, jnp.float32)
+    contrib = {}
     for step_x in (-1, 0, 1):
-        if step_x == 1:
-            slab = jnp.concatenate([lower_plane, gathered[:, : planes - 1]], axis=1)
-        elif step_x == -1:
-            slab = jnp.concatenate([gathered[:, 1:], upper_plane], axis=1)
-        else:
-            slab = gathered
         first = 9 * (step_x + 1)
+        total = None
         for step_y in (-1, 0, 1):
             kernel = weight[first + step_y + 1 : first + 9 : 3].reshape(3 * channels, outputs)
             product = jnp.einsum(
-                "bxzcy,kc->bxzky", slab, kernel, preferred_element_type=jnp.float32
+                "bxzcy,kc->bxzky", gathered, kernel, preferred_element_type=jnp.float32
             )
             for place, step_z in enumerate((-1, 0, 1)):
-                part = product[:, :, :, place * channels : (place + 1) * channels]
-                accum = accum + shift_cells(part, step_z, step_y)
+                part = shift_cells(product[:, :, :, place * channels : (place + 1) * channels], step_z, step_y)
+                total = part if total is None else total + part
+        contrib[step_x] = total
+    from_prev = from_behind(contrib[1][:, -1:], "space", 1)
+    from_next = from_behind(contrib[-1][:, :1], "space", -1)
+    accum = (
+        contrib[0]
+        + jnp.concatenate([from_prev, contrib[1][:, : planes - 1]], axis=1)
+        + jnp.concatenate([contrib[-1][:, 1:], from_next], axis=1)
+    )
     input_grad = accum.astype(jnp.bfloat16)
     return (input_grad, weight_grad)
 

time: 128 us -> 113 us (0.88)
  starting transfers between devices: 32.1 us -> 22.5 us
  local copies, waits for them, and re-layouts: 19.8 us -> 15.3 us
  other arithmetic: 6.83 us -> 4 us
  waiting for transfers between devices: 42.8 us -> 44.2 us
    all_gather x1 -> x0, waiting for transfers between devices: 14.5 us -> none  [local(): halo = lax.all_gather(cot_halo, 'chan', axis=3, tiled=True)]
    all_gather x1, waiting for transfers between devices: 0.01 us -> 8.97 us  [local(): gathered = lax.all_gather(cotangent, 'chan', axis=3, tiled=True)]
    ppermute x5, starting transfers between devices: 13 us -> 5.4 us  [exchange_sum(): lax.ppermute(value, axis, [(i, i ^ distance) for i in range(count)])]
    ppermute x5, waiting for transfers between devices: 27 us -> 33.7 us  [exchange_sum(): lax.ppermute(value, axis, [(i, i ^ distance) for i in range(count)])]
    slice x8, local copies, waits for them, and re-layouts: 6.61 us -> 2.08 us  [the longest x6 2 us: local(): product[:, :, :, place * channels:(place + 1) * channels]]
    convert_element_type x1, other arithmetic: 4.32 us -> 1.52 us  [local(): input_grad = accum.astype(jnp.bfloat16)]
    ppermute x4, starting transfers between devices: 19.1 us -> 17.1 us  [from_behind(): lax.ppermute(value, axis, [(source, source + steps) for source in range(i...]
    add x0 -> x2, other arithmetic: none -> 1.63 us  [local(): total = part if total is None else total + part]
  transfers between devices with their start and end apart: 11 -> 10, of which waited for: 6 -> 7; matrix products, arithmetic and copies ran while one was open for 29% -> 20% of each run, Pallas kernels for 0% -> 0%
where the time goes in v3:
time: 113 us; the launch traced here: 112 us
  waiting for transfers between devices  44.2 us (39%)
  starting transfers between devices  22.5 us (20%)
  local copies, waits for them, and re-layouts  15.3 us (14%)
  between operations  14.3 us (13%)
  matrix products  11.9 us (11%)
  other arithmetic  4 us (4%)
    ppermute x5, waiting for transfers between devices, exchange_sum(): lax.ppermute(value, axis, [(i, i ^ distance) for i in range(count)])  33.7 us
    ppermute x4, starting transfers between devices, from_behind(): lax.ppermute(value, axis, [(source, source + steps) for source in range(i...  17.1 us
    unnamed x16, local copies, waits for them, and re-layouts  10.3 us
    all_gather x1, waiting for transfers between devices, local(): gathered = lax.all_gather(cotangent, 'chan', axis=3, tiled=True)  8.97 us
    dot_general x3, matrix products, local(): jnp.einsum('bxzky,bxzcy->kc', source, gathered, preferred_element_type=jn...  8.07 us
    ppermute x5, starting transfers between devices, exchange_sum(): lax.ppermute(value, axis, [(i, i ^ distance) for i in range(count)])  5.4 us
    dot_general x9, matrix products, local(): jnp.einsum('bxzcy,kc->bxzky', gathered, kernel, preferred_element_type=jn...  3.82 us
  transfers between devices with their start and end apart: 10, of which 7 were waited for; matrix products, arithmetic and copies ran while one was open for 20% of the time, Pallas kernels for 0%

profile of v3, /device:TPU:4, one launch (start us, length us, event | category | flops | bytes accessed | tf_op | source)
XLA Modules:
  0.0 112.2 jit_solution(3024075588676889384)
XLA Ops:
  7.9 1.0 fusion.106
  8.9 3.8 %collective-permute-start.2 = (bf16[1,1,8,16,512]{4,3,2,1,0:T(8,128)(2,1)S(1)}, bf16[1,1,8,16,512]{4,3,2,1,0:T(8,128)(2,1)S(1)}, u32[]{:S(2)}, u32[]{:S(2)}) collective-permute-start(bf16[1,1,8,16,512]{4,3,2,1,0:T(8,128)(2,1)S(1)} %get-tuple-element.31), channel_id=1, source_target_pairs={{0,16},{16,32},{32,48},{48,64},{64,80},{80,96},{96,112},{112,128},... | collective-permute-start | bytes 393224 | tf_op jit(solution)/shard_map/ppermute | solution.py:12
  12.7 5.8 %collective-permute-start.3 = (bf16[1,1,8,16,512]{4,3,2,1,0:T(8,128)(2,1)S(1)}, bf16[1,1,8,16,512]{4,3,2,1,0:T(8,128)(2,1)S(1)}, u32[]{:S(2)}, u32[]{:S(2)}) collective-permute-start(bf16[1,1,8,16,512]{4,3,2,1,0:T(8,128)(2,1)S(1)} %get-tuple-element.30), channel_id=1, source_target_pairs={{16,0},{32,16},{48,32},{64,48},{80,64},{96,80},{112,96},{128,112},... | collective-permute-start | bytes 393224 | tf_op jit(solution)/shard_map/ppermute | solution.py:12
  18.5 0.9 fusion.107
  19.4 0.7 collective-permute-done.2
  20.1 1.0 constant_dynamic-update-slice_fusion.1
  21.3 1.0 fusion.91
  22.3 0.9 fusion.60
  23.2 1.1 fusion.92
  24.3 1.2 %fusion.83 = bf16[1,4,8,144,512]{4,3,2,1,0:T(8,128)(2,1)} fusion(bf16[1,4,8,144,512]{4,3,2,1,0:T(8,128)(2,1)} %fusion.92, bf16[1,4,8,16,512]{4,3,2,1,0:T(8,128)(2,1)S(1)} %constant_dynamic-update-slice_fusion), kind=kLoop, calls=%fused_computation.94 | loop fusion | bytes 1048576
  26.1 0.7 constant_dynamic-update-slice_fusion.4
  26.9 0.7 constant_dynamic-update-slice_fusion.3
  27.6 1.1 %fusion.84 = bf16[1,4,8,144,512]{4,3,2,1,0:T(8,128)(2,1)} fusion(bf16[1,4,8,144,512]{4,3,2,1,0:T(8,128)(2,1)} %constant_dynamic-update-slice_fusion.3, bf16[1,4,8,16,512]{4,3,2,1,0:T(8,128)(2,1)S(1)} %constant_dynamic-update-slice_fusion), kind=kLoop, calls=%fused_computation.95 | loop fusion | bytes 1048576
  28.7 1.0 fusion.93
  29.7 0.9 fusion.61
  30.6 1.1 fusion.94
  31.7 9.0 %all-gather.2.cloned.1.call-done = bf16[1,2,8,128,512]{4,3,2,1,0:T(8,128)(2,1)} async-done(((bf16[1,2,8,16,512]{4,3,2,1,0:T(8,128)(2,1)}), bf16[1,2,8,128,512]{4,3,2,1,0:T(8,128)(2,1)}) %all-gather.2.cloned.1.call-update) | async-done | bytes 2097168 | tf_op jit(solution)/shard_map/all_gather | solution.py:40
  40.6 3.2 %fusion.51 = f32[144,128]{1,0:T(8,128)S(1)} fusion(bf16[1,2,8,128,512]{4,3,2,1,0:T(8,128)(2,1)} %all-gather.2.cloned.1.call-done, bf16[1,4,8,144,512]{4,3,2,1,0:T(8,128)(2,1)} %fusion.94), kind=kOutput, calls=%fused_computation.36 | convolution fusion | flops 301989888 | bytes 4530176 | tf_op jit(solution)/shard_map/bxzky,bxzcy->kc/dot_general | solution.py:49
  43.9 2.4 %fusion.54 = f32[144,128]{1,0:T(8,128)S(1)} fusion(bf16[1,2,8,128,512]{4,3,2,1,0:T(8,128)(2,1)S(1)} %copy-done, bf16[1,4,8,144,512]{4,3,2,1,0:T(8,128)(2,1)} %fusion.94), kind=kOutput, calls=%fused_computation.37 | convolution fusion | flops 301989888 | bytes 4530176 | tf_op jit(solution)/shard_map/bxzky,bxzcy->kc/dot_general | solution.py:49
  46.3 2.4 %fusion.57 = f32[144,128]{1,0:T(8,128)S(1)} fusion(bf16[1,2,8,128,512]{4,3,2,1,0:T(8,128)(2,1)S(1)} %copy-done, bf16[1,4,8,144,512]{4,3,2,1,0:T(8,128)(2,1)} %fusion.94), kind=kOutput, calls=%fused_computation.38 | convolution fusion | flops 301989888 | bytes 4530176 | tf_op jit(solution)/shard_map/bxzky,bxzcy->kc/dot_general | solution.py:49
  48.8 1.3 %collective-permute-start.4 = (f32[27,16,128]{2,1,0:T(8,128)S(1)}, f32[27,16,128]{2,1,0:T(8,128)S(1)}, u32[]{:S(2)}, u32[]{:S(2)}) collective-permute-start(f32[27,16,128]{2,1,0:T(8,128)S(1)} %bitcast.167), channel_id=1, source_target_pairs={{0,1},{1,0},{2,3},{3,2},{4,5},{5,4},{6,7},{7,6},{8,9},{9,8},{10,11... | collective-permute-start | bytes 663560 | tf_op jit(solution)/shard_map/ppermute | solution.py:17
  52.0 0.8 fusion.82
  52.9 5.5 %collective-permute-start.1 = (f32[1,1,8,16,512]{4,3,2,1,0:T(8,128)S(1)}, f32[1,1,8,16,512]{4,3,2,1,0:T(8,128)S(1)}, u32[]{:S(2)}, u32[]{:S(2)}) collective-permute-start(f32[1,1,8,16,512]{4,3,2,1,0:T(8,128)S(1)} %get-tuple-element.27), channel_id=1, source_target_pairs={{16,0},{32,16},{48,32},{64,48},{80,64},{96,80},{112,96},{128,112},... | collective-permute-start | bytes 786440 | tf_op jit(solution)/shard_map/ppermute | solution.py:12
  60.3 0.8 fusion.76
  61.2 1.9 %collective-permute-start = (f32[1,1,8,16,512]{4,3,2,1,0:T(8,128)S(1)}, f32[1,1,8,16,512]{4,3,2,1,0:T(8,128)S(1)}, u32[]{:S(2)}, u32[]{:S(2)}) collective-permute-start(f32[1,1,8,16,512]{4,3,2,1,0:T(8,128)S(1)} %get-tuple-element.28), channel_id=1, source_target_pairs={{0,16},{16,32},{32,48},{48,64},{64,80},{80,96},{96,112},{112,128},... | collective-permute-start | bytes 786440 | tf_op jit(solution)/shard_map/ppermute | solution.py:12
  64.1 9.4 %collective-permute-done.5 = f32[27,16,128]{2,1,0:T(8,128)S(1)} collective-permute-done((f32[27,16,128]{2,1,0:T(8,128)S(1)}, f32[27,16,128]{2,1,0:T(8,128)S(1)}, u32[]{:S(2)}, u32[]{:S(2)}) %collective-permute-start.5) | collective-permute-done | bytes 221216 | tf_op jit(solution)/shard_map/ppermute | solution.py:17
  74.6 6.9 %collective-permute-done.6 = f32[27,16,128]{2,1,0:T(8,128)S(1)} collective-permute-done((f32[27,16,128]{2,1,0:T(8,128)S(1)}, f32[27,16,128]{2,1,0:T(8,128)S(1)}, u32[]{:S(2)}, u32[]{:S(2)}) %collective-permute-start.6) | collective-permute-done | bytes 221216 | tf_op jit(solution)/shard_map/ppermute | solution.py:17
  82.2 10.7 %collective-permute-done.7 = f32[27,16,128]{2,1,0:T(8,128)S(1)} collective-permute-done((f32[27,16,128]{2,1,0:T(8,128)S(1)}, f32[27,16,128]{2,1,0:T(8,128)S(1)}, u32[]{:S(2)}, u32[]{:S(2)}) %collective-permute-start.7) | collective-permute-done | bytes 221216 | tf_op jit(solution)/shard_map/ppermute | solution.py:17
  92.9 3.4 %collective-permute-start.8 = (f32[27,16,128]{2,1,0:T(8,128)S(1)}, f32[27,16,128]{2,1,0:T(8,128)S(1)}, u32[]{:S(2)}, u32[]{:S(2)}) collective-permute-start(f32[27,16,128]{2,1,0:T(8,128)S(1)} %add.186), channel_id=1, source_target_pairs={{0,64},{16,80},{32,96},{48,112},{64,0},{80,16},{96,32},{112,48},{1... | collective-permute-start | bytes 663560 | tf_op jit(solution)/shard_map/ppermute | solution.py:17
  96.4 1.5 %fusion.70 = bf16[1,2,8,16,512]{4,3,2,1,0:T(8,128)(2,1)} fusion(f32[1,2,8,16,512]{4,3,2,1,0:T(8,128)S(1)} %get-tuple-element.25, f32[1,2,8,16,512]{4,3,2,1,0:T(8,128)S(1)} %get-tuple-element.24, f32[1,2,8,16,512]{4,3,2,1,0:T(8,128)S(1)} %get-tuple-element.48, f32[1,2,8,16,512]{4,3,2,1,0:T(8,128)S(1)} %get-tuple-element.19, ...), kind=kLoop, calls=%fused_computation.81 | loop fusion | flops 1703936 | bytes 6029312 | tf_op jit(solution)/shard_map/convert_element_type | solution.py:76
  97.9 6.7 %collective-permute-done.8 = f32[27,16,128]{2,1,0:T(8,128)S(1)} collective-permute-done((f32[27,16,128]{2,1,0:T(8,128)S(1)}, f32[27,16,128]{2,1,0:T(8,128)S(1)}, u32[]{:S(2)}, u32[]{:S(2)}) %collective-permute-start.8) | collective-permute-done | bytes 221216 | tf_op jit(solution)/shard_map/ppermute | solution.py:17
  104.6 0.7 add_multiply_fusion
  (38 shorter events, 8.3 us)
Async XLA Ops:
  7.2 33.5 %all-gather.2.cloned.1.call-start = ((), (), s32[]{:S(2)}) async-start(), calls=%async_computation | async-start | bytes 2359296 | tf_op jit(solution)/shard_map/all_gather | solution.py:40
  8.9 11.2 %collective-permute-start.2 = (bf16[1,1,8,16,512]{4,3,2,1,0:T(8,128)(2,1)S(1)}, bf16[1,1,8,16,512]{4,3,2,1,0:T(8,128)(2,1)S(1)}, u32[]{:S(2)}, u32[]{:S(2)}) collective-permute-start(bf16[1,1,8,16,512]{4,3,2,1,0:T(8,128)(2,1)S(1)} %get-tuple-element.31), channel_id=1, source_target_pairs={{0,16},{16,32},{32,48},{48,64},{64,80},{80,96},{96,112},{112,128},... | collective-permute-start | bytes 393224 | tf_op jit(solution)/shard_map/ppermute | solution.py:12
  12.7 8.5 %collective-permute-start.3 = (bf16[1,1,8,16,512]{4,3,2,1,0:T(8,128)(2,1)S(1)}, bf16[1,1,8,16,512]{4,3,2,1,0:T(8,128)(2,1)S(1)}, u32[]{:S(2)}, u32[]{:S(2)}) collective-permute-start(bf16[1,1,8,16,512]{4,3,2,1,0:T(8,128)(2,1)S(1)} %get-tuple-element.30), channel_id=1, source_target_pairs={{16,0},{32,16},{48,32},{64,48},{80,64},{96,80},{112,96},{128,112},... | collective-permute-start | bytes 393224 | tf_op jit(solution)/shard_map/ppermute | solution.py:12
  21.3 4.8 %copy-start.1 = (bf16[1,2,8,16,512]{4,3,2,1,0:T(8,128)(2,1)S(1)}, bf16[1,2,8,16,512]{4,3,2,1,0:T(8,128)(2,1)}, u32[]{:S(2)}) copy-start(bf16[1,2,8,16,512]{4,3,2,1,0:T(8,128)(2,1)} %param.3) | copy-start | bytes 786436
  40.6 3.2 %copy-start = (bf16[1,2,8,128,512]{4,3,2,1,0:T(8,128)(2,1)S(1)}, bf16[1,2,8,128,512]{4,3,2,1,0:T(8,128)(2,1)}, u32[]{:S(2)}) copy-start(bf16[1,2,8,128,512]{4,3,2,1,0:T(8,128)(2,1)} %all-gather.2.cloned.1.call-done) | copy-start | bytes 6291460
  48.8 14.4 %collective-permute-start.4 = (f32[27,16,128]{2,1,0:T(8,128)S(1)}, f32[27,16,128]{2,1,0:T(8,128)S(1)}, u32[]{:S(2)}, u32[]{:S(2)}) collective-permute-start(f32[27,16,128]{2,1,0:T(8,128)S(1)} %bitcast.167), channel_id=1, source_target_pairs={{0,1},{1,0},{2,3},{3,2},{4,5},{5,4},{6,7},{7,6},{8,9},{9,8},{10,11... | collective-permute-start | bytes 663560 | tf_op jit(solution)/shard_map/ppermute | solution.py:17
  52.9 43.5 %collective-permute-start.1 = (f32[1,1,8,16,512]{4,3,2,1,0:T(8,128)S(1)}, f32[1,1,8,16,512]{4,3,2,1,0:T(8,128)S(1)}, u32[]{:S(2)}, u32[]{:S(2)}) collective-permute-start(f32[1,1,8,16,512]{4,3,2,1,0:T(8,128)S(1)} %get-tuple-element.27), channel_id=1, source_target_pairs={{16,0},{32,16},{48,32},{64,48},{80,64},{96,80},{112,96},{128,112},... | collective-permute-start | bytes 786440 | tf_op jit(solution)/shard_map/ppermute | solution.py:12
  61.2 35.1 %collective-permute-start = (f32[1,1,8,16,512]{4,3,2,1,0:T(8,128)S(1)}, f32[1,1,8,16,512]{4,3,2,1,0:T(8,128)S(1)}, u32[]{:S(2)}, u32[]{:S(2)}) collective-permute-start(f32[1,1,8,16,512]{4,3,2,1,0:T(8,128)S(1)} %get-tuple-element.28), channel_id=1, source_target_pairs={{0,16},{16,32},{32,48},{48,64},{64,80},{80,96},{96,112},{112,128},... | collective-permute-start | bytes 786440 | tf_op jit(solution)/shard_map/ppermute | solution.py:12
  63.2 10.3 %collective-permute-start.5 = (f32[27,16,128]{2,1,0:T(8,128)S(1)}, f32[27,16,128]{2,1,0:T(8,128)S(1)}, u32[]{:S(2)}, u32[]{:S(2)}) collective-permute-start(f32[27,16,128]{2,1,0:T(8,128)S(1)} %add.183), channel_id=1, source_target_pairs={{0,16},{16,0},{32,48},{48,32},{64,80},{80,64},{96,112},{112,96},{1... | collective-permute-start | bytes 663560 | tf_op jit(solution)/shard_map/ppermute | solution.py:17
  73.5 8.0 %collective-permute-start.6 = (f32[27,16,128]{2,1,0:T(8,128)S(1)}, f32[27,16,128]{2,1,0:T(8,128)S(1)}, u32[]{:S(2)}, u32[]{:S(2)}) collective-permute-start(f32[27,16,128]{2,1,0:T(8,128)S(1)} %add.184), channel_id=1, source_target_pairs={{0,128},{16,144},{32,160},{48,176},{64,192},{80,208},{96,224},{112... | collective-permute-start | bytes 663560 | tf_op jit(solution)/shard_map/ppermute | solution.py:17
  81.6 11.3 %collective-permute-start.7 = (f32[27,16,128]{2,1,0:T(8,128)S(1)}, f32[27,16,128]{2,1,0:T(8,128)S(1)}, u32[]{:S(2)}, u32[]{:S(2)}) collective-permute-start(f32[27,16,128]{2,1,0:T(8,128)S(1)} %add.185), channel_id=1, source_target_pairs={{0,32},{16,48},{32,0},{48,16},{64,96},{80,112},{96,64},{112,80},{1... | collective-permute-start | bytes 663560 | tf_op jit(solution)/shard_map/ppermute | solution.py:17
  92.9 11.7 %collective-permute-start.8 = (f32[27,16,128]{2,1,0:T(8,128)S(1)}, f32[27,16,128]{2,1,0:T(8,128)S(1)}, u32[]{:S(2)}, u32[]{:S(2)}) collective-permute-start(f32[27,16,128]{2,1,0:T(8,128)S(1)} %add.186), channel_id=1, source_target_pairs={{0,64},{16,80},{32,96},{48,112},{64,0},{80,16},{96,32},{112,48},{1... | collective-permute-start | bytes 663560 | tf_op jit(solution)/shard_map/ppermute | solution.py:17
Sparse Core Ops, SparseCore 0:
  9.8 30.7 all-gather.1
